TPU v7x, 256 devices: a whole 4x4x8 slice. The times are simulated.
256 devices in a mesh: ctx: 64 (over y, z, core), ch: 4 (over x).
Axes of the slice: x: 4, y: 4, z: 8, core: 2. Of those that a mesh axis runs over, the one named last changes fastest.
Arguments:
- tokens: bfloat16 [16384, 4096], P('ctx', 'ch'), may hold values from -6 to 6
- in_weight: bfloat16 [3, 4096, 4096], P(None, 'ctx', 'ch'), may hold values from -0.09375 to 0.09375
- short_taps: float32 [3, 3, 4096], P(None, None, 'ch'), may hold values from -4 to 4
- long_filter: float32 [4, 1024, 16384], P('ch', 'ctx'), may hold values from -0.046875 to 0.046875
- skip_gain: float32 [4, 1024], P('ch', 'ctx'), may hold values from 0.25 to 2
Outputs:
- gated_output: bfloat16 [4096, 16384], P('ch', 'ctx')
All inputs are finite; a program needn't handle non-finite values.
Results may differ from a plain program's by a relative error of at most 0.015.
Values may be sent and summed in bfloat16 or wider, within the bound.
No kernel may reach another device: no remote copies, remote signals or barrier semaphores. Data moves between devices by JAX's collectives and lax.ppermute only.
A program may use at most 128 MiB of HBM per device.

v0:
```python
import math
import jax
import jax.numpy as jnp
from jax import lax
import numpy as np
from jax.sharding import Mesh, NamedSharding
from jax.sharding import PartitionSpec as P

BLOCK = 1024
FACTOR = 32


def shifted(block, axis, size, distance):
    route = [(i - distance, i) for i in range(size) if 0 <= i - distance < size]
    return lax.ppermute(block, axis, route)


def unit_wave(rows, cols, period, scale_rows):
    outer = rows // FACTOR
    hi = jnp.arange(outer, dtype=jnp.int32)[:, None] * (FACTOR * scale_rows)
    lo = jnp.arange(FACTOR, dtype=jnp.int32)[:, None] * scale_rows
    col = jnp.arange(cols, dtype=jnp.int32)[None, :]
    step = 2.0 * math.pi / period
    hi_phase = step * (hi * col % period).astype(jnp.float32)
    lo_phase = step * (lo * col % period).astype(jnp.float32)
    hc, hs = (jnp.cos(hi_phase)[:, None, :], jnp.sin(hi_phase)[:, None, :])
    lc, ls = (jnp.cos(lo_phase)[None, :, :], jnp.sin(lo_phase)[None, :, :])
    cos_t = (hc * lc - hs * ls).reshape(rows, cols)
    sin_t = (hs * lc + hc * ls).reshape(rows, cols)
    return (cos_t, sin_t)


def spectral_tables(tile_extent):
    period = 2 * tile_extent
    cos_f, sin_f = unit_wave(tile_extent, tile_extent, period, 1)
    alternating = jnp.where(jnp.arange(tile_extent) % 2 == 0, 1.0, -1.0).astype(jnp.float32)
    first_col = (jnp.arange(tile_extent) == 0)[None, :]
    forward = jnp.concatenate(
        [cos_f, jnp.where(first_col, alternating[:, None], -sin_f)], axis=1
    ).astype(jnp.bfloat16)
    cos_b, sin_b = unit_wave(tile_extent, period, period, 1)
    first_row = (jnp.arange(tile_extent) == 0)[:, None]
    alt_t = jnp.where(jnp.arange(period) % 2 == 0, 1.0, -1.0).astype(jnp.float32)[None, :]
    weights = jnp.where(first_row, 1.0, 2.0) / period
    inverse = jnp.concatenate(
        [weights * cos_b, jnp.where(first_row, alt_t / period, -(2.0 / period) * sin_b)], axis=0
    ).astype(jnp.bfloat16)
    return (forward, inverse)


def filter_spectra(kernel_table_lines, forward, tile_extent):
    lane_total, context_extent = kernel_table_lines.shape
    groups = context_extent // tile_extent
    kernel = (
        kernel_table_lines.astype(jnp.bfloat16)
        .reshape(lane_total, groups, tile_extent)
        .transpose(1, 0, 2)
        .reshape(groups * lane_total, tile_extent)
    )
    spec_k = jnp.dot(kernel, forward, preferred_element_type=jnp.float32)
    return spec_k.reshape(groups, lane_total, 2 * tile_extent)


def global_causal_smear(gate_wave, spec_k, leftover_lines, forward, inverse, tile_extent):
    lane_total, context_extent = gate_wave.shape
    groups = context_extent // tile_extent
    slot0 = (jnp.arange(tile_extent) == 0)[None, None, :]
    source = gate_wave.reshape(lane_total * groups, tile_extent)
    spec_x = jnp.dot(source, forward, preferred_element_type=jnp.float32)
    spec_x = spec_x.reshape(lane_total, groups, 2 * tile_extent)
    x_re, x_im = (spec_x[:, :, :tile_extent], spec_x[:, :, tile_extent:])
    k_re, k_im = (spec_k[:, :, :tile_extent], spec_k[:, :, tile_extent:])
    pad = jnp.zeros((lane_total, groups - 1, tile_extent), jnp.float32)
    xp_re = jnp.concatenate([pad, x_re], axis=1)
    xp_im = jnp.concatenate([pad, x_im], axis=1)
    rr = ii = ri = ir = None
    for offset in range(groups):
        s_re = xp_re[:, groups - 1 - offset : 2 * groups - 1 - offset]
        s_im = xp_im[:, groups - 1 - offset : 2 * groups - 1 - offset]
        f_re = k_re[offset][:, None, :]
        f_im = k_im[offset][:, None, :]
        terms = (f_re * s_re, f_im * s_im, f_re * s_im, f_im * s_re)
        if rr is None:
            rr, ii, ri, ir = terms
        else:
            rr, ii, ri, ir = (rr + terms[0], ii + terms[1], ri + terms[2], ir + terms[3])
    y_re = rr - jnp.where(slot0, 0.0, ii)
    y_im = jnp.where(slot0, ii, ri + ir)
    packed = jnp.concatenate([y_re, y_im], axis=2).astype(jnp.bfloat16)
    rows = jnp.dot(
        packed.reshape(lane_total * groups, 2 * tile_extent),
        inverse,
        preferred_element_type=jnp.float32,
    ).reshape(lane_total, groups, 2 * tile_extent)
    front_half = rows[:, :, :tile_extent]
    back_half = rows[:, :, tile_extent:]
    carried = jnp.concatenate(
        [jnp.zeros((lane_total, 1, tile_extent), jnp.float32), back_half[:, :-1]], axis=1
    )
    affine_mapping = (front_half + carried).reshape(lane_total, context_extent)
    wide = gate_wave.astype(jnp.float32)
    return (affine_mapping + leftover_lines[:, None] * wide).astype(jnp.bfloat16)


def short_conv(projected_float, local_taps, previous):
    context_extent = projected_float.shape[2]
    extended = jnp.concatenate([previous, projected_float], axis=2)
    result = jnp.zeros_like(projected_float)
    for offset in range(3):
        result = (
            result
            + local_taps[:, offset, :][:, :, None]
            * extended[:, :, 2 - offset : 2 - offset + context_extent]
        )
    return result


def make_shards(n_ctx, n_ch, tile_extent):
    ctx = ("yh", "cq")
    swap = [(0, 1), (1, 0)]

    def featured(projected, taps):
        local_tokens = projected.shape[2]
        previous = shifted(projected[:, :, local_tokens - 2 :], ctx, n_ctx, 1)
        return short_conv(projected.astype(jnp.float32), taps, previous.astype(jnp.float32))

    def by_half(half, own, other):
        first = jnp.where(half == 0, own, other)
        second = jnp.where(half == 0, other, own)
        return jnp.stack([first, second])

    def shards(tokens, in_weight, short_taps, long_filter, skip_gain):
        half = lax.axis_index("yh")
        local_tokens, local_features = tokens.shape
        branches, local_rows, lanes = in_weight.shape
        width = lanes // 2
        n_q = n_ctx // 2
        own_cols = lax.dynamic_slice_in_dim(in_weight, half * width, width, axis=2)
        other_cols = lax.dynamic_slice_in_dim(in_weight, (1 - half) * width, width, axis=2)
        partner_rows = lax.ppermute(other_cols, "yh", swap)
        rows_pair = jnp.stack(list(by_half(half, own_cols, partner_rows)), axis=1)
        gathered = lax.all_gather(rows_pair, "cq", axis=2, tiled=False)
        whole_weight = gathered.reshape(branches, -1, width)
        partner_tokens = lax.ppermute(tokens, "yh", swap)
        token_pair = by_half(half, tokens, partner_tokens)
        copies = jnp.broadcast_to(token_pair[None], (n_ch,) + token_pair.shape)
        pieces = lax.all_to_all(copies, "ch", split_axis=0, concat_axis=3, tiled=True)
        whole_tokens = pieces.reshape(2 * local_tokens, n_ch * local_features)
        forward, inverse = spectral_tables(tile_extent)
        spec_k = filter_spectra(long_filter[0], forward, tile_extent)
        whole_weight, forward, inverse, spec_k = lax.optimization_barrier(
            (whole_weight, forward, inverse, spec_k)
        )
        summed = jnp.einsum(
            "pdc,ld->pcl", whole_weight, whole_tokens, preferred_element_type=jnp.float32
        ).astype(jnp.bfloat16)
        own_part = lax.dynamic_slice_in_dim(summed[0:1], half * local_tokens, local_tokens, axis=2)
        other_part = lax.dynamic_slice_in_dim(
            summed[0:1], (1 - half) * local_tokens, local_tokens, axis=2
        )
        received = lax.ppermute(other_part, "yh", swap)
        q = lax.axis_index("cq")
        blocks = summed[1:3].reshape(2, width, 2, local_tokens)
        tails = blocks[:, :, :, local_tokens - 2 :].transpose(0, 2, 3, 1).reshape(-1, width)
        ring = [(i, (i + 1) % n_q) for i in range(n_q)]
        arrived = lax.ppermute(tails, "cq", ring).reshape(2, 2, 2, width).transpose(0, 3, 1, 2)
        first = jnp.concatenate([jnp.zeros_like(arrived[:, :, :1]), arrived[:, :, :1]], axis=2)
        halo = jnp.where(q == 0, first, arrived)
        taps12 = lax.dynamic_slice_in_dim(short_taps[1:3], half * width, width, axis=2)
        extended = jnp.concatenate([halo, blocks], axis=3).astype(jnp.float32)
        embed12 = None
        for offset in range(3):
            term = (
                taps12[:, offset, :][:, :, None, None]
                * extended[:, :, :, 2 - offset : 2 - offset + local_tokens]
            )
            embed12 = term if embed12 is None else embed12 + term
        gate_wave = (embed12[0] * embed12[1]).astype(jnp.bfloat16)
        lanes_each = width // n_q
        outgoing12 = gate_wave.reshape(n_q, lanes_each, 2, local_tokens)
        got = lax.all_to_all(outgoing12, "cq", split_axis=0, concat_axis=0, tiled=True)
        received, got = lax.optimization_barrier((received, got))
        per_channel_view = got.transpose(1, 2, 0, 3).reshape(lanes_each, -1)
        projected0 = jnp.concatenate(list(by_half(half, own_part, received)), axis=1)
        embed0 = featured(projected0, short_taps[0:1])
        blended_lines = global_causal_smear(
            per_channel_view, spec_k, skip_gain[0], forward, inverse, tile_extent
        )
        lines, span = blended_lines.shape
        outgoing = blended_lines.reshape(lines, n_ctx, span // n_ctx).transpose(1, 0, 2)
        returned = lax.all_to_all(outgoing, ctx, split_axis=0, concat_axis=0, tiled=True)
        by_token = returned.reshape(n_ctx * lines, span // n_ctx)
        gated_output = (embed0[0] * by_token.astype(jnp.float32)).astype(jnp.bfloat16)
        return gated_output

    return shards


def solution(mesh):
    n_ctx = mesh.shape["ctx"]
    grid = np.asarray(mesh.devices).reshape(2, n_ctx // 2, mesh.shape["ch"])
    split_mesh = Mesh(grid, ("yh", "cq", "ch"))
    ctx = ("yh", "cq")
    placed = (
        P(ctx, "ch"),
        P(None, ctx, "ch"),
        P(None, None, "ch"),
        P("ch", ctx, None),
        P("ch", ctx),
    )
    mapped = jax.shard_map(
        make_shards(n_ctx, mesh.shape["ch"], BLOCK),
        mesh=split_mesh,
        in_specs=placed,
        out_specs=P("ch", ctx),
        check_vma=False,
    )
    out_sharding = NamedSharding(mesh, P("ch", "ctx"))

    def run(*args):
        return lax.with_sharding_constraint(mapped(*args), out_sharding)

    return run
```

profile of v0, /device:TPU:1, one launch (start us, length us, event | category | flops | bytes accessed | tf_op | source)
XLA Modules:
  0.0 207.8 jit_solution(14225138241267218314)
XLA Ops:
  6.5 1.0 constant_dynamic-slice_fusion.4
  7.5 3.8 %collective-permute-start = (bf16[3,64,512]{2,1,0:T(8,128)(2,1)S(1)}, bf16[3,64,512]{2,1,0:T(8,128)(2,1)S(1)}, u32[]{:S(2)}, u32[]{:S(2)}) collective-permute-start(bf16[3,64,512]{2,1,0:T(8,128)(2,1)S(1)} %constant_dynamic-slice_fusion.4), channel_id=1, source_target_pairs={{0,128},{128,0},{1,129},{129,1},{2,130},{130,2},{3,131},{131,3},{4... | collective-permute-start | bytes 589832 | tf_op jit(solution)/shard_map/ppermute | solution.py:140
  11.3 3.6 %collective-permute-done = bf16[3,64,512]{2,1,0:T(8,128)(2,1)S(1)} collective-permute-done((bf16[3,64,512]{2,1,0:T(8,128)(2,1)S(1)}, bf16[3,64,512]{2,1,0:T(8,128)(2,1)S(1)}, u32[]{:S(2)}, u32[]{:S(2)}) %collective-permute-start) | collective-permute-done | bytes 196640 | tf_op jit(solution)/shard_map/ppermute | solution.py:140
  14.9 1.0 select_bitcast_fusion.3
  15.9 0.8 pad_maximum_fusion.5
  16.7 3.8 %collective-permute-start.1 = (bf16[256,1024]{1,0:T(8,128)(2,1)}, bf16[256,1024]{1,0:T(8,128)(2,1)}, u32[]{:S(2)}, u32[]{:S(2)}) collective-permute-start(bf16[256,1024]{1,0:T(8,128)(2,1)} %param.5), channel_id=1, source_target_pairs={{0,128},{128,0},{1,129},{129,1},{2,130},{130,2},{3,131},{131,3},{4... | collective-permute-start | bytes 1572872 | tf_op jit(solution)/shard_map/ppermute | solution.py:144
  20.5 1.3 convert_element_type.115
  21.8 0.3 copy.37
  22.1 1.1 copy.24
  23.3 0.5 fusion.52
  23.9 0.6 fusion.55
  24.4 1.0 fusion.42
  25.5 0.8 add_negate_fusion
  26.3 0.8 subtract_convert_fusion
  27.1 0.3 fusion.6
  27.4 2.6 %pad_maximum_fusion.1 = bf16[1024,2048]{1,0:T(8,128)(2,1)} fusion(bf16[1024,1024]{1,0:T(8,128)(2,1)S(1)} %fusion.6, bf16[1024,1024]{1,0:T(8,128)(2,1)S(1)} %bitcast.149), kind=kLoop, calls=%fused_computation.39 | loop fusion | flops 8388608 | bytes 8388608 | tf_op jit(solution)/shard_map/concatenate | solution.py:38
  30.0 1.1 fusion.45
  31.1 3.5 %add_multiply_fusion = bf16[32,32,2048]{2,1,0:T(8,128)(2,1)} fusion(f32[32,2048]{1,0:T(8,128)S(1)} %get-tuple-element.69, f32[32,2048]{1,0:T(8,128)S(1)} %get-tuple-element.64, f32[32,2048]{1,0:T(8,128)S(1)} %get-tuple-element.70, f32[32,2048]{1,0:T(8,128)S(1)} %get-tuple-element.63), kind=kLoop, calls=%fused_computation.7 | loop fusion | flops 10485760 | bytes 5242880 | tf_op jit(solution)/shard_map/mul | solution.py:46
  34.7 1.1 select_bitcast_fusion.1
  35.9 2.5 %broadcast_in_dim.111 = bf16[4,2,256,1024]{3,2,1,0:T(8,128)(2,1)} broadcast(bf16[2,256,1024]{2,1,0:T(8,128)(2,1)S(1)} %pad_maximum_fusion.3), dimensions={1,2,3} | broadcast | bytes 5242880 | tf_op jit(solution)/shard_map/broadcast_in_dim | solution.py:146
  38.4 5.1 %all-to-all-start = ((bf16[4,2,256,1024]{3,2,1,0:T(8,128)(2,1)}), bf16[4,2,256,1024]{3,2,1,0:T(8,128)(2,1)}, u32[]{:S(2)}, u32[]{:S(2)}) async-start(bf16[4,2,256,1024]{3,2,1,0:T(8,128)(2,1)} %broadcast_in_dim.111), calls=%async_computation | async-start | bytes 8388608 | tf_op jit(solution)/shard_map/all_to_all | solution.py:147
  43.5 4.5 %fusion.67 = f32[2048,256]{0,1:T(8,128)} fusion(bf16[256,1024]{1,0:T(8,128)(2,1)} %bitcast.159, bf16[1024,1024]{1,0:T(8,128)(2,1)} %copy-done.1, bf16[1024,1024]{1,0:T(8,128)(2,1)S(1)} %bitcast.150), kind=kOutput, calls=%fused_computation.195 | convolution fusion | flops 1082130432 | bytes 6815744 | tf_op jit(solution)/shard_map/dot_general | solution.py:60
  48.0 2.9 %fusion.2 = bf16[1024,2048]{1,0:T(8,128)(2,1)} fusion(bf16[32,32,2048]{2,1,0:T(8,128)(2,1)S(1)} %copy-done, bf16[2048]{0:T(1024)(128)(2,1)S(1)} %select_multiply_fusion, pred[1024]{0:T(1024)(128)(4,1)S(1)} %iota_compare_fusion), kind=kLoop, calls=%fused_computation.4 | loop fusion | flops 2097152 | bytes 8393728 | tf_op jit(solution)/shard_map/convert.5 | solution.py:221
  50.9 1.2 multiply_subtract_fusion
  52.1 2.5 %fusion.3 = bf16[1024,2048]{1,0:T(8,128)(2,1)} fusion(f32[32,32,2048]{2,1,0:T(8,128)S(1)} %multiply_subtract_fusion, f32[1024]{0:T(1024)S(1)} %select_multiply_fusion.1), kind=kLoop, calls=%fused_computation.6 | loop fusion | flops 4194304 | bytes 12587008 | tf_op jit(solution)/shard_map/convert.4 | solution.py:221
  54.6 8.5 %pad_maximum_fusion = bf16[2048,2048]{1,0:T(8,128)(2,1)} fusion(bf16[1024,2048]{1,0:T(8,128)(2,1)} %fusion.2, bf16[1024,2048]{1,0:T(8,128)(2,1)} %fusion.3), kind=kLoop, calls=%fused_computation | loop fusion | flops 16777216 | bytes 16777216 | tf_op jit(solution)/shard_map/concatenate | solution.py:45
  63.1 27.3 %all-to-all-done = bf16[4,2,256,1024]{3,2,1,0:T(8,128)(2,1)} async-done(((bf16[4,2,256,1024]{3,2,1,0:T(8,128)(2,1)}), bf16[4,2,256,1024]{3,2,1,0:T(8,128)(2,1)}, u32[]{:S(2)}, u32[]{:S(2)}) %all-to-all-start) | async-done | bytes 4194336 | tf_op jit(solution)/shard_map/all_to_all | solution.py:147
  90.4 7.4 %copy.25 = bf16[1,2,256,4,1024]{4,3,2,1,0:T(4,128)(2,1)} copy(bf16[1,2,256,4,1024]{4,2,1,3,0:T(8,128)(2,1)} %bitcast.16) | data formatting | bytes 8388608 | tf_op jit(solution)/shard_map/all_to_all | solution.py:147
  97.8 7.8 %reshape.442 = bf16[512,4096,1]{1,0,2:T(8,128)(2,1)} reshape(bf16[1,2,256,4,1024]{4,3,2,1,0:T(4,128)(2,1)} %copy.25) | data formatting | bytes 8388608 | tf_op jit(solution)/shard_map/reshape | solution.py:148
  105.7 10.9 %convolution_convert_fusion = bf16[3,512,512]{1,2,0:T(8,128)(2,1)S(1)} fusion(bf16[512,4096,1]{1,0,2:T(8,128)(2,1)} %reshape.442, bf16[3,4096,512]{2,1,0:T(8,128)(2,1)} %bitcast.166), kind=kOutput, calls=%fused_computation.51 | convolution fusion | flops 6443237376 | bytes 18350080 | tf_op jit(solution)/shard_map/pdc,ld->pcl/dot_general | solution.py:154
  116.6 1.2 copy-done.5
  117.8 4.5 %collective-permute-start.3 = (bf16[8,512]{1,0:T(8,128)(2,1)S(1)}, bf16[8,512]{1,0:T(8,128)(2,1)S(1)}, u32[]{:S(2)}, u32[]{:S(2)}) collective-permute-start(bf16[8,512]{1,0:T(8,128)(2,1)S(1)} %reshape.435), channel_id=1, source_target_pairs={{0,4},{4,8},{8,12},{12,16},{16,20},{20,24},{24,28},{28,32},{32,36}... | collective-permute-start | bytes 24584 | tf_op jit(solution)/shard_map/ppermute | solution.py:166
  122.4 0.5 copy.27
  122.9 0.2 collective-permute-done.3
  123.2 0.3 copy.26
  123.5 0.7 maximum_convert_fusion
  124.2 1.7 fusion.7
  126.0 0.9 copy.28
  126.8 10.7 %all-to-all-start.1 = ((bf16[32,16,2,256]{3,1,2,0:T(8,128)(2,1)}), bf16[32,16,2,256]{3,1,2,0:T(8,128)(2,1)S(1)}, u32[]{:S(2)}, u32[]{:S(2)}) async-start(bf16[32,16,2,256]{3,1,2,0:T(8,128)(2,1)} %copy.28), calls=%async_computation.1 | async-start | bytes 1048576 | tf_op jit(solution)/shard_map/all_to_all | solution.py:181
  137.6 1.1 slice.381
  138.6 0.8 copy-done.2
  139.5 1.6 collective-permute-start.2
  141.1 0.9 slice_bitcast_fusion.30
  142.0 0.8 slice_bitcast_fusion.31
  142.8 9.8 %collective-permute-done.2 = bf16[1,512,256]{1,2,0:T(8,128)(2,1)} collective-permute-done((bf16[1,512,256]{1,2,0:T(8,128)(2,1)S(1)}, bf16[1,512,256]{1,2,0:T(8,128)(2,1)}, u32[]{:S(2)}, u32[]{:S(2)}) %collective-permute-start.2) | collective-permute-done | bytes 262176 | tf_op jit(solution)/shard_map/ppermute | solution.py:161
  152.6 1.5 all-to-all-done.1
  154.1 0.3 copy.29
  154.4 0.3 dot_general.19
  154.9 3.6 %fusion.4 = f32[16,16,2048]{2,1,0:T(8,128)S(1)} fusion(bf16[16,16,1024]{2,1,0:T(8,128)(2,1)S(1)} %dot_general.19, bf16[1024,2048]{1,0:T(8,128)(2,1)} %pad_maximum_fusion.1), kind=kOutput, calls=%fused_computation.40 | convolution fusion | flops 1073741824 | bytes 6815744 | tf_op jit(solution)/shard_map/dot_general | solution.py:69
  158.6 0.2 fusion.68
  159.0 4.5 %subtract_convert_fusion.1 = bf16[16,16,1024]{2,1,0:T(8,128)(2,1)S(1)} fusion(f32[16,16,1024]{2,1,0:T(8,128)S(1)} %get-tuple-element.50, f32[16,1024]{1,0:T(8,128)S(1)} %copy-done.9, f32[16,1024]{1,0:T(8,128)S(1)} %copy-done.10, f32[16,1024]{1,0:T(8,128)S(1)} %copy-done.12, f32[16,1024]{1,0:T(8,128)S(1)} %copy-done.13, f32[16,1024]{1,0:T(8,128)S(1)} %copy-done.14, ...), kind=kLoop, calls=%fused_computation.75 | loop fusion | flops 17039360 | bytes 4719616 | tf_op jit(solution)/shard_map/convert.2 | solution.py:221
  163.6 5.2 %select_convert_fusion = bf16[16,16,1024]{2,1,0:T(8,128)(2,1)S(1)} fusion(f32[16,16,1024]{2,1,0:T(8,128)S(1)} %get-tuple-element.50, f32[16,16,1024]{2,1,0:T(8,128)S(1)} %get-tuple-element.49, f32[16,1024]{1,0:T(8,128)S(1)} %get-tuple-element.18, f32[16,1024]{1,0:T(8,128)S(1)} %get-tuple-element.19, f32[16,1024]{1,0:T(8,128)S(1)} %get-tuple-element.20, ...), kind=kLoop, calls=%fused_computation.74 | loop fusion | flops 25165824 | bytes 4719616 | tf_op jit(solution)/shard_map/convert.3 | solution.py:221
  168.9 2.4 %fusion = f32[16,16,2048]{2,1,0:T(8,128)S(1)} fusion(bf16[2048,2048]{1,0:T(8,128)(2,1)S(1)} %bitcast.148, bf16[16,16,1024]{2,1,0:T(8,128)(2,1)S(1)} %select_convert_fusion, bf16[16,16,1024]{2,1,0:T(8,128)(2,1)S(1)} %subtract_convert_fusion.1), kind=kOutput, calls=%fused_computation.1 | convolution fusion | flops 2149580800 | bytes 11534336 | tf_op jit(solution)/shard_map/dot_general | solution.py:90
  171.4 0.2 slice_add_fusion
  171.6 0.3 reshape.437
  172.1 1.4 fusion.22
  173.5 8.1 %all-to-all-start.2 = ((bf16[64,16,256]{2,1,0:T(8,128)(2,1)}), bf16[64,16,256]{2,1,0:T(8,128)(2,1)S(1)}, u32[]{:S(2)}, u32[]{:S(2)}) async-start(bf16[64,16,256]{2,1,0:T(8,128)(2,1)} %bitcast.61), calls=%async_computation.2 | async-start | bytes 1048576 | tf_op jit(solution)/shard_map/all_to_all | solution.py:191
  181.6 1.0 broadcast_select_fusion
  182.7 3.5 %collective-permute-start.4 = (bf16[1,1024,2]{1,2,0:T(2,128)(2,1)S(1)}, bf16[1,1024,2]{1,2,0:T(2,128)(2,1)S(1)}, u32[]{:S(2)}, u32[]{:S(2)}) collective-permute-start(bf16[1,1024,2]{1,2,0:T(2,128)(2,1)S(1)} %fusion.60), channel_id=1, source_target_pairs={{0,4},{4,8},{8,12},{12,16},{16,20},{20,24},{24,28},{28,32},{32,36}... | collective-permute-start | bytes 12296 | tf_op jit(solution)/shard_map/ppermute | solution.py:15
  186.4 3.7 %collective-permute-done.4 = bf16[1,1024,2]{1,2,0:T(2,128)(2,1)S(1)} collective-permute-done((bf16[1,1024,2]{1,2,0:T(2,128)(2,1)S(1)}, bf16[1,1024,2]{1,2,0:T(2,128)(2,1)S(1)}, u32[]{:S(2)}, u32[]{:S(2)}) %collective-permute-start.4) | collective-permute-done | bytes 4128 | tf_op jit(solution)/shard_map/ppermute | solution.py:15
  190.1 9.0 %all-to-all-done.2 = bf16[64,16,256]{2,1,0:T(8,128)(2,1)S(1)} async-done(((bf16[64,16,256]{2,1,0:T(8,128)(2,1)}), bf16[64,16,256]{2,1,0:T(8,128)(2,1)S(1)}, u32[]{:S(2)}, u32[]{:S(2)}) %all-to-all-start.2) | async-done | bytes 524320 | tf_op jit(solution)/shard_map/all_to_all | solution.py:191
  199.2 0.3 copy.32
  199.6 0.4 fusion.15
  199.9 1.0 copy.33
  (88 shorter events, 1.2 us)
Async XLA Ops:
  6.5 16.7 %slice-start.2 = ((f32[3,3,1024]{2,1,0:T(4,128)}), f32[2,3,1024]{2,1,0:T(4,128)S(1)}, s32[]{:S(2)}) async-start(f32[3,3,1024]{2,1,0:T(4,128)} %param.7), calls=%async_computation.6 | async-start | bytes 65536 | tf_op jit(solution)/shard_map/slice | solution.py:169
  6.5 99.1 %all-gather.3.cloned.1.call-start = ((), (), s32[]{:S(2)}) async-start(), calls=%async_computation.3 | async-start | bytes 12976128 | tf_op jit(solution)/shard_map/all_gather | solution.py:142
  7.5 7.4 %collective-permute-start = (bf16[3,64,512]{2,1,0:T(8,128)(2,1)S(1)}, bf16[3,64,512]{2,1,0:T(8,128)(2,1)S(1)}, u32[]{:S(2)}, u32[]{:S(2)}) collective-permute-start(bf16[3,64,512]{2,1,0:T(8,128)(2,1)S(1)} %constant_dynamic-slice_fusion.4), channel_id=1, source_target_pairs={{0,128},{128,0},{1,129},{129,1},{2,130},{130,2},{3,131},{131,3},{4... | collective-permute-start | bytes 589832 | tf_op jit(solution)/shard_map/ppermute | solution.py:140
  16.7 18.0 %collective-permute-start.1 = (bf16[256,1024]{1,0:T(8,128)(2,1)}, bf16[256,1024]{1,0:T(8,128)(2,1)}, u32[]{:S(2)}, u32[]{:S(2)}) collective-permute-start(bf16[256,1024]{1,0:T(8,128)(2,1)} %param.5), channel_id=1, source_target_pairs={{0,128},{128,0},{1,129},{129,1},{2,130},{130,2},{3,131},{131,3},{4... | collective-permute-start | bytes 1572872 | tf_op jit(solution)/shard_map/ppermute | solution.py:144
  27.4 2.6 %copy-start.1 = (bf16[1024,1024]{1,0:T(8,128)(2,1)}, bf16[1024,1024]{1,0:T(8,128)(2,1)S(1)}, u32[]{:S(2)}) copy-start(bf16[1024,1024]{1,0:T(8,128)(2,1)S(1)} %fusion.6) | copy-start | bytes 6291460
  30.0 4.6 %copy-start.24 = (bf16[256,1024]{1,0:T(8,128)(2,1)S(1)}, bf16[256,1024]{1,0:T(8,128)(2,1)}, u32[]{:S(2)}) copy-start(bf16[256,1024]{1,0:T(8,128)(2,1)} %param.5) | copy-start | bytes 1572868
  38.4 52.0 %all-to-all-start = ((bf16[4,2,256,1024]{3,2,1,0:T(8,128)(2,1)}), bf16[4,2,256,1024]{3,2,1,0:T(8,128)(2,1)}, u32[]{:S(2)}, u32[]{:S(2)}) async-start(bf16[4,2,256,1024]{3,2,1,0:T(8,128)(2,1)} %broadcast_in_dim.111), calls=%async_computation | async-start | bytes 8388608 | tf_op jit(solution)/shard_map/all_to_all | solution.py:147
  43.5 4.5 %copy-start = (bf16[32,32,2048]{2,1,0:T(8,128)(2,1)S(1)}, bf16[32,32,2048]{2,1,0:T(8,128)(2,1)}, u32[]{:S(2)}) copy-start(bf16[32,32,2048]{2,1,0:T(8,128)(2,1)} %add_multiply_fusion) | copy-start | bytes 12582916
  116.6 1.2 copy-start.5
  117.8 5.3 %collective-permute-start.3 = (bf16[8,512]{1,0:T(8,128)(2,1)S(1)}, bf16[8,512]{1,0:T(8,128)(2,1)S(1)}, u32[]{:S(2)}, u32[]{:S(2)}) collective-permute-start(bf16[8,512]{1,0:T(8,128)(2,1)S(1)} %reshape.435), channel_id=1, source_target_pairs={{0,4},{4,8},{8,12},{12,16},{16,20},{20,24},{24,28},{28,32},{32,36}... | collective-permute-start | bytes 24584 | tf_op jit(solution)/shard_map/ppermute | solution.py:166
  125.8 15.2 %copy-start.4 = (f32[2048,256]{0,1:T(8,128)S(1)}, f32[2048,256]{0,1:T(8,128)}, u32[]{:S(2)}) copy-start(f32[2048,256]{0,1:T(8,128)} %fusion.67) | copy-start | bytes 6291460
  126.8 27.3 %all-to-all-start.1 = ((bf16[32,16,2,256]{3,1,2,0:T(8,128)(2,1)}), bf16[32,16,2,256]{3,1,2,0:T(8,128)(2,1)S(1)}, u32[]{:S(2)}, u32[]{:S(2)}) async-start(bf16[32,16,2,256]{3,1,2,0:T(8,128)(2,1)} %copy.28), calls=%async_computation.1 | async-start | bytes 1048576 | tf_op jit(solution)/shard_map/all_to_all | solution.py:181
  138.6 0.8 copy-start.2
  139.5 13.1 %collective-permute-start.2 = (bf16[1,512,256]{1,2,0:T(8,128)(2,1)S(1)}, bf16[1,512,256]{1,2,0:T(8,128)(2,1)}, u32[]{:S(2)}, u32[]{:S(2)}) collective-permute-start(bf16[1,512,256]{1,2,0:T(8,128)(2,1)S(1)} %constant_dynamic-slice_fusion.3), channel_id=1, source_target_pairs={{0,128},{128,0},{1,129},{129,1},{2,130},{130,2},{3,131},{131,3},{4... | collective-permute-start | bytes 786440 | tf_op jit(solution)/shard_map/ppermute | solution.py:161
  154.8 4.1 %copy-start.6 = (f32[16,1024]{1,0:T(8,128)S(1)}, f32[16,1024]{1,0:T(8,128)}, u32[]{:S(2)}) copy-start(f32[16,1024]{1,0:T(8,128)} %get-tuple-element.31) | copy-start | bytes 196612
  154.8 4.1 %copy-start.7 = (f32[16,1024]{1,0:T(8,128)S(1)}, f32[16,1024]{1,0:T(8,128)}, u32[]{:S(2)}) copy-start(f32[16,1024]{1,0:T(8,128)} %get-tuple-element.32) | copy-start | bytes 196612
  154.8 4.1 %copy-start.8 = (f32[16,1024]{1,0:T(8,128)S(1)}, f32[16,1024]{1,0:T(8,128)}, u32[]{:S(2)}) copy-start(f32[16,1024]{1,0:T(8,128)} %get-tuple-element.33) | copy-start | bytes 196612
  154.8 4.1 %copy-start.9 = (f32[16,1024]{1,0:T(8,128)S(1)}, f32[16,1024]{1,0:T(8,128)}, u32[]{:S(2)}) copy-start(f32[16,1024]{1,0:T(8,128)} %get-tuple-element.34) | copy-start | bytes 196612
  154.8 4.1 %copy-start.10 = (f32[16,1024]{1,0:T(8,128)S(1)}, f32[16,1024]{1,0:T(8,128)}, u32[]{:S(2)}) copy-start(f32[16,1024]{1,0:T(8,128)} %get-tuple-element.35) | copy-start | bytes 196612
  154.8 4.1 %copy-start.11 = (f32[16,1024]{1,0:T(8,128)S(1)}, f32[16,1024]{1,0:T(8,128)}, u32[]{:S(2)}) copy-start(f32[16,1024]{1,0:T(8,128)} %get-tuple-element.36) | copy-start | bytes 196612
  154.8 4.1 %copy-start.12 = (f32[16,1024]{1,0:T(8,128)S(1)}, f32[16,1024]{1,0:T(8,128)}, u32[]{:S(2)}) copy-start(f32[16,1024]{1,0:T(8,128)} %get-tuple-element.37) | copy-start | bytes 196612
  154.8 4.1 %copy-start.13 = (f32[16,1024]{1,0:T(8,128)S(1)}, f32[16,1024]{1,0:T(8,128)}, u32[]{:S(2)}) copy-start(f32[16,1024]{1,0:T(8,128)} %get-tuple-element.38) | copy-start | bytes 196612
  154.8 4.1 %copy-start.14 = (f32[16,1024]{1,0:T(8,128)S(1)}, f32[16,1024]{1,0:T(8,128)}, u32[]{:S(2)}) copy-start(f32[16,1024]{1,0:T(8,128)} %get-tuple-element.39) | copy-start | bytes 196612
  154.8 4.1 %copy-start.15 = (f32[16,1024]{1,0:T(8,128)S(1)}, f32[16,1024]{1,0:T(8,128)}, u32[]{:S(2)}) copy-start(f32[16,1024]{1,0:T(8,128)} %get-tuple-element.40) | copy-start | bytes 196612
  154.9 4.1 %copy-start.16 = (f32[16,1024]{1,0:T(8,128)S(1)}, f32[16,1024]{1,0:T(8,128)}, u32[]{:S(2)}) copy-start(f32[16,1024]{1,0:T(8,128)} %get-tuple-element.41) | copy-start | bytes 196612
  154.9 4.1 %copy-start.17 = (f32[16,1024]{1,0:T(8,128)S(1)}, f32[16,1024]{1,0:T(8,128)}, u32[]{:S(2)}) copy-start(f32[16,1024]{1,0:T(8,128)} %get-tuple-element.42) | copy-start | bytes 196612
  154.9 4.1 %copy-start.18 = (f32[16,1024]{1,0:T(8,128)S(1)}, f32[16,1024]{1,0:T(8,128)}, u32[]{:S(2)}) copy-start(f32[16,1024]{1,0:T(8,128)} %get-tuple-element.43) | copy-start | bytes 196612
  154.9 4.1 %copy-start.19 = (f32[16,1024]{1,0:T(8,128)S(1)}, f32[16,1024]{1,0:T(8,128)}, u32[]{:S(2)}) copy-start(f32[16,1024]{1,0:T(8,128)} %get-tuple-element.44) | copy-start | bytes 196612
  154.9 4.1 %copy-start.20 = (f32[16,1024]{1,0:T(8,128)S(1)}, f32[16,1024]{1,0:T(8,128)}, u32[]{:S(2)}) copy-start(f32[16,1024]{1,0:T(8,128)} %get-tuple-element.45) | copy-start | bytes 196612
  154.9 4.1 %copy-start.21 = (f32[16,1024]{1,0:T(8,128)S(1)}, f32[16,1024]{1,0:T(8,128)}, u32[]{:S(2)}) copy-start(f32[16,1024]{1,0:T(8,128)} %get-tuple-element.46) | copy-start | bytes 196612
  154.9 4.1 %copy-start.22 = (f32[16,1024]{1,0:T(8,128)S(1)}, f32[16,1024]{1,0:T(8,128)}, u32[]{:S(2)}) copy-start(f32[16,1024]{1,0:T(8,128)} %get-tuple-element.47) | copy-start | bytes 196612
  154.9 4.1 %copy-start.23 = (f32[16,1024]{1,0:T(8,128)S(1)}, f32[16,1024]{1,0:T(8,128)}, u32[]{:S(2)}) copy-start(f32[16,1024]{1,0:T(8,128)} %get-tuple-element.48) | copy-start | bytes 196612
  158.6 10.4 %slice-start = ((s8[8388608]{0:T(1024)(128)(4,1)}), s8[4194304]{0:T(1024)(128)(4,1)S(1)}, s32[]{:S(2)}) async-start(s8[8388608]{0:T(1024)(128)(4,1)} %bitcast.147), calls=%async_computation.4 | async-start | bytes 8388608
  159.0 9.9 %slice-start.1 = ((s8[8388608]{0:T(1024)(128)(4,1)}), s8[4194304]{0:T(1024)(128)(4,1)S(1)}, s32[]{:S(2)}) async-start(s8[8388608]{0:T(1024)(128)(4,1)} %bitcast.147), calls=%async_computation.5 | async-start | bytes 8388608
  171.4 0.7 copy-start.26
  171.6 10.0 %copy-start.25 = (f32[3,3,1024]{2,1,0:T(4,128)S(1)}, f32[3,3,1024]{2,1,0:T(4,128)}, u32[]{:S(2)}) copy-start(f32[3,3,1024]{2,1,0:T(4,128)} %param.7) | copy-start | bytes 110596
  171.9 9.7 %copy-start.3 = (bf16[1,512,512]{1,2,0:T(8,128)(2,1)S(1)}, bf16[1,512,512]{1,2,0:T(8,128)(2,1)}, u32[]{:S(2)}) copy-start(bf16[1,512,512]{1,2,0:T(8,128)(2,1)} %copy-done.2) | copy-start | bytes 1572868
  173.5 25.6 %all-to-all-start.2 = ((bf16[64,16,256]{2,1,0:T(8,128)(2,1)}), bf16[64,16,256]{2,1,0:T(8,128)(2,1)S(1)}, u32[]{:S(2)}, u32[]{:S(2)}) async-start(bf16[64,16,256]{2,1,0:T(8,128)(2,1)} %bitcast.61), calls=%async_computation.2 | async-start | bytes 1048576 | tf_op jit(solution)/shard_map/all_to_all | solution.py:191
  182.7 7.4 %collective-permute-start.4 = (bf16[1,1024,2]{1,2,0:T(2,128)(2,1)S(1)}, bf16[1,1024,2]{1,2,0:T(2,128)(2,1)S(1)}, u32[]{:S(2)}, u32[]{:S(2)}) collective-permute-start(bf16[1,1024,2]{1,2,0:T(2,128)(2,1)S(1)} %fusion.60), channel_id=1, source_target_pairs={{0,4},{4,8},{8,12},{12,16},{16,20},{20,24},{24,28},{28,32},{32,36}... | collective-permute-start | bytes 12296 | tf_op jit(solution)/shard_map/ppermute | solution.py:15
Sparse Core Ops, SparseCore 0:
  16.8 84.7 all-gather.2
where the time goes:
time: 209 us; the launch traced here: 208 us
  waiting for transfers between devices  55.2 us (26%)
  other arithmetic  46.3 us (22%)
  starting transfers between devices  41.1 us (20%)
  local copies, waits for them, and re-layouts  29.6 us (14%)
  matrix products  21.4 us (10%)
  between operations  14.2 us (7%)
    all_to_all x1, waiting for transfers between devices, shards(): lax.all_to_all(copies, 'ch', split_axis=0, concat_axis=3, tiled=True)  27.3 us
    another operation x6, other arithmetic, run(): return lax.with_sharding_constraint(mapped(*args), out_sharding)  16.2 us
    dot_general x1, matrix products, shards(): jnp.einsum('pdc,ld->pcl', whole_weight, whole_tokens, preferred_element_t...  10.9 us
    all_to_all x1, starting transfers between devices, shards(): lax.all_to_all(outgoing12, 'cq', split_axis=0, concat_axis=0, tiled=True)  10.7 us
    ppermute x1, waiting for transfers between devices, shards(): received = lax.ppermute(other_part, 'yh', swap)  9.8 us
    all_to_all x1, waiting for transfers between devices, shards(): lax.all_to_all(outgoing, ctx, split_axis=0, concat_axis=0, tiled=True)  9.01 us
    concatenate x1, other arithmetic, spectral_tables(): jnp.concatenate([weights * cos_b, jnp.where(first_row, alt_t / period, -(...  8.5 us
    all_to_all x1, starting transfers between devices, shards(): lax.all_to_all(outgoing, ctx, split_axis=0, concat_axis=0, tiled=True)  8.09 us
  transfers between devices with their start and end apart: 9, of which 7 were waited for; matrix products, arithmetic and copies ran while one was open for 28% of the time, Pallas kernels for 0%

commit v1 on v0

--- a/solution.py
+++ b/solution.py
@@ -144,7 +144,18 @@
         partner_tokens = lax.ppermute(tokens, "yh", swap)
         token_pair = by_half(half, tokens, partner_tokens)
         copies = jnp.broadcast_to(token_pair[None], (n_ch,) + token_pair.shape)
-        pieces = lax.all_to_all(copies, "ch", split_axis=0, concat_axis=3, tiled=True)
+        ways, here = (lax.axis_size("ch"), lax.axis_index("ch"))
+        width_2 = copies.shape[0] // ways
+        shape = list(copies.shape)
+        shape[0] = width_2
+        height = shape[3]
+        shape[3] = height * ways
+        pieces = jnp.zeros(shape, copies.dtype)
+        for mask in range(ways):
+            part = lax.dynamic_slice_in_dim(copies, (here ^ mask) * width_2, width_2, axis=0)
+            if mask:
+                part = lax.ppermute(part, "ch", [(d, d ^ mask) for d in range(ways)])
+            pieces = lax.dynamic_update_slice_in_dim(pieces, part, (here ^ mask) * height, axis=3)
         whole_tokens = pieces.reshape(2 * local_tokens, n_ch * local_features)
         forward, inverse = spectral_tables(tile_extent)
         spec_k = filter_spectra(long_filter[0], forward, tile_extent)

time: 209 us -> 201 us (0.962)
  local copies, waits for them, and re-layouts: 29.6 us -> 18.1 us
  waiting for transfers between devices: 55.2 us -> 65.4 us
  starting transfers between devices: 41.1 us -> 36.9 us
    ppermute x0 -> x3, waiting for transfers between devices: none -> 31.8 us  [shards(): part = lax.ppermute(part, 'ch', [(d, d ^ mask) for d in range(ways)])]
    all_to_all x1 -> x0, waiting for transfers between devices: 27.3 us -> none  [shards(): lax.all_to_all(copies, 'ch', split_axis=0, concat_axis=3, tiled=True)]
    reshape x1 -> x0, local copies, waits for them, and re-layouts: 7.81 us -> none  [shards(): whole_tokens = pieces.reshape(2 * local_tokens, n_ch * local_features)]
    all_to_all x1 -> x0, local copies, waits for them, and re-layouts: 7.43 us -> none  [shards(): lax.all_to_all(copies, 'ch', split_axis=0, concat_axis=3, tiled=True)]
    all_gather x1, waiting for transfers between devices: 0.01 us -> 7.12 us  [shards(): gathered = lax.all_gather(rows_pair, 'cq', axis=2, tiled=False)]
    all_to_all x1 -> x0, starting transfers between devices: 5.06 us -> none  [shards(): lax.all_to_all(copies, 'ch', split_axis=0, concat_axis=3, tiled=True)]
    dynamic_update_slice x0 -> x3, local copies, waits for them, and re-layouts: none -> 4.52 us  [shards(): lax.dynamic_update_slice_in_dim(pieces, part, (here ^ mask) * height, axi...]
    ppermute x0 -> x3, starting transfers between devices: none -> 3.95 us  [shards(): part = lax.ppermute(part, 'ch', [(d, d ^ mask) for d in range(ways)])]
  transfers between devices with their start and end apart: 9 -> 11, of which waited for: 7 -> 10; matrix products, arithmetic and copies ran while one was open for 28% -> 21% of each run, Pallas kernels for 0% -> 0%
where the time goes in v1:
time: 201 us; the launch traced here: 200 us
  waiting for transfers between devices  65.4 us (33%)
  other arithmetic  45.2 us (22%)
  starting transfers between devices  36.9 us (18%)
  matrix products  20.4 us (10%)
  local copies, waits for them, and re-layouts  18.1 us (9%)
  between operations  14.1 us (7%)
    ppermute x3, waiting for transfers between devices, shards(): part = lax.ppermute(part, 'ch', [(d, d ^ mask) for d in range(ways)])  31.8 us
    another operation x6, other arithmetic, run(): return lax.with_sharding_constraint(mapped(*args), out_sharding)  16.2 us
    dot_general x1, matrix products, shards(): jnp.einsum('pdc,ld->pcl', whole_weight, whole_tokens, preferred_element_t...  11.7 us
    all_to_all x1, waiting for transfers between devices, shards(): lax.all_to_all(outgoing, ctx, split_axis=0, concat_axis=0, tiled=True)  9.01 us
    all_to_all x1, starting transfers between devices, shards(): lax.all_to_all(outgoing, ctx, split_axis=0, concat_axis=0, tiled=True)  8.8 us
    ppermute x1, waiting for transfers between devices, shards(): received = lax.ppermute(other_part, 'yh', swap)  8.67 us
    concatenate x1, other arithmetic, spectral_tables(): jnp.concatenate([weights * cos_b, jnp.where(first_row, alt_t / period, -(...  8.54 us
    all_to_all x1, starting transfers between devices, shards(): lax.all_to_all(outgoing12, 'cq', split_axis=0, concat_axis=0, tiled=True)  8.4 us
  transfers between devices with their start and end apart: 11, of which 10 were waited for; matrix products, arithmetic and copies ran while one was open for 21% of the time, Pallas kernels for 0%

profile of v1, /device:TPU:1, one launch (start us, length us, event | category | flops | bytes accessed | tf_op | source)
XLA Modules:
  0.0 200.1 jit_solution(15073103764078163453)
XLA Ops:
  6.5 0.9 constant_dynamic-slice_fusion.4
  7.5 3.8 %collective-permute-start = (bf16[3,64,512]{2,1,0:T(8,128)(2,1)S(1)}, bf16[3,64,512]{2,1,0:T(8,128)(2,1)S(1)}, u32[]{:S(2)}, u32[]{:S(2)}) collective-permute-start(bf16[3,64,512]{2,1,0:T(8,128)(2,1)S(1)} %constant_dynamic-slice_fusion.4), channel_id=1, source_target_pairs={{0,128},{128,0},{1,129},{129,1},{2,130},{130,2},{3,131},{131,3},{4... | collective-permute-start | bytes 589832 | tf_op jit(solution)/shard_map/ppermute | solution.py:140
  11.3 3.6 %collective-permute-done = bf16[3,64,512]{2,1,0:T(8,128)(2,1)S(1)} collective-permute-done((bf16[3,64,512]{2,1,0:T(8,128)(2,1)S(1)}, bf16[3,64,512]{2,1,0:T(8,128)(2,1)S(1)}, u32[]{:S(2)}, u32[]{:S(2)}) %collective-permute-start) | collective-permute-done | bytes 196640 | tf_op jit(solution)/shard_map/ppermute | solution.py:140
  14.9 1.0 select_bitcast_fusion.3
  15.9 0.8 pad_maximum_fusion.4
  16.7 3.8 %collective-permute-start.1 = (bf16[256,1024]{1,0:T(8,128)(2,1)}, bf16[256,1024]{1,0:T(8,128)(2,1)S(1)}, u32[]{:S(2)}, u32[]{:S(2)}) collective-permute-start(bf16[256,1024]{1,0:T(8,128)(2,1)} %param.5), channel_id=1, source_target_pairs={{0,128},{128,0},{1,129},{129,1},{2,130},{130,2},{3,131},{131,3},{4... | collective-permute-start | bytes 1572872 | tf_op jit(solution)/shard_map/ppermute | solution.py:144
  20.5 1.3 convert_element_type.115
  22.1 0.3 copy.24
  22.4 0.5 fusion.52
  23.0 0.6 fusion.55
  23.6 1.0 fusion.42
  24.6 0.8 add_negate_fusion
  25.4 0.8 subtract_convert_fusion
  26.2 0.3 fusion.6
  26.6 2.6 %fusion.67 = f32[2048,256]{0,1:T(8,128)} fusion(bf16[256,1024]{1,0:T(8,128)(2,1)S(1)} %bitcast.163, bf16[1024,1024]{1,0:T(8,128)(2,1)S(1)} %fusion.6, bf16[1024,1024]{1,0:T(8,128)(2,1)S(1)} %bitcast.153), kind=kOutput, calls=%fused_computation.199 | convolution fusion | flops 1082130432 | bytes 6815744 | tf_op jit(solution)/shard_map/dot_general | solution.py:60
  29.2 1.1 fusion.45
  30.3 1.6 add_multiply_fusion
  31.9 1.3 multiply_subtract_fusion
  33.2 2.5 %fusion.3 = bf16[1024,2048]{1,0:T(8,128)(2,1)} fusion(f32[32,32,2048]{2,1,0:T(8,128)S(1)} %multiply_subtract_fusion, f32[1024]{0:T(1024)S(1)} %select_multiply_fusion.1), kind=kLoop, calls=%fused_computation.6 | loop fusion | flops 4194304 | bytes 12587008 | tf_op jit(solution)/shard_map/convert.4 | solution.py:232
  35.6 2.8 %fusion.2 = bf16[1024,2048]{1,0:T(8,128)(2,1)} fusion(bf16[32,32,2048]{2,1,0:T(8,128)(2,1)S(1)} %add_multiply_fusion, bf16[2048]{0:T(1024)(128)(2,1)S(1)} %select_multiply_fusion, pred[1024]{0:T(1024)(128)(4,1)S(1)} %iota_compare_fusion), kind=kLoop, calls=%fused_computation.4 | loop fusion | flops 2097152 | bytes 8393728 | tf_op jit(solution)/shard_map/convert.5 | solution.py:232
  38.5 1.1 maximum_bitcast_fusion
  39.6 1.2 collective-permute-start.2
  40.9 2.4 %pad_maximum_fusion.1 = bf16[1024,2048]{1,0:T(8,128)(2,1)} fusion(bf16[1024,1024]{1,0:T(8,128)(2,1)S(1)} %fusion.6, bf16[1024,1024]{1,0:T(8,128)(2,1)S(1)} %bitcast.154), kind=kLoop, calls=%fused_computation.39 | loop fusion | flops 8388608 | bytes 8388608 | tf_op jit(solution)/shard_map/concatenate | solution.py:38
  43.3 2.5 %collective-permute-start.3 = (bf16[1,2,256,1024]{3,2,1,0:T(8,128)(2,1)}, bf16[1,2,256,1024]{3,2,1,0:T(8,128)(2,1)S(1)}, u32[]{:S(2)}, u32[]{:S(2)}) collective-permute-start(bf16[1,2,256,1024]{3,2,1,0:T(8,128)(2,1)} %maximum_bitcast_fusion), channel_id=1, source_target_pairs={{0,2},{1,3},{2,0},{3,1},{4,6},{5,7},{6,4},{7,5},{8,10},{9,11},{10,... | collective-permute-start | bytes 3145736 | tf_op jit(solution)/shard_map/ppermute | solution.py:157
  46.1 8.5 %pad_maximum_fusion = bf16[2048,2048]{1,0:T(8,128)(2,1)} fusion(bf16[1024,2048]{1,0:T(8,128)(2,1)} %fusion.2, bf16[1024,2048]{1,0:T(8,128)(2,1)} %fusion.3), kind=kLoop, calls=%fused_computation | loop fusion | flops 16777216 | bytes 16777216 | tf_op jit(solution)/shard_map/concatenate | solution.py:45
  54.6 2.6 %broadcast_in_dim.114 = bf16[1,2,256,4096]{3,2,1,0:T(8,128)(2,1)} broadcast(bf16[]{:T(256)} %constant.104.clone.1), dimensions={} | broadcast | bytes 4194306 | tf_op jit(solution)/shard_map/broadcast_in_dim | solution.py:153
  57.2 1.1 constant_dynamic-update-slice_fusion.3
  58.3 4.6 %collective-permute-done.2 = bf16[1,2,256,1024]{3,2,1,0:T(8,128)(2,1)S(1)} collective-permute-done((bf16[1,2,256,1024]{3,2,1,0:T(8,128)(2,1)}, bf16[1,2,256,1024]{3,2,1,0:T(8,128)(2,1)S(1)}, u32[]{:S(2)}, u32[]{:S(2)}) %collective-permute-start.2) | collective-permute-done | bytes 1048608 | tf_op jit(solution)/shard_map/ppermute | solution.py:157
  62.9 1.1 constant_dynamic-update-slice_fusion.2
  63.9 23.5 %collective-permute-done.3 = bf16[1,2,256,1024]{3,2,1,0:T(8,128)(2,1)S(1)} collective-permute-done((bf16[1,2,256,1024]{3,2,1,0:T(8,128)(2,1)}, bf16[1,2,256,1024]{3,2,1,0:T(8,128)(2,1)S(1)}, u32[]{:S(2)}, u32[]{:S(2)}) %collective-permute-start.3) | collective-permute-done | bytes 1048608 | tf_op jit(solution)/shard_map/ppermute | solution.py:157
  87.5 1.1 constant_dynamic-update-slice_fusion.1
  88.6 3.6 %collective-permute-done.4 = bf16[1,2,256,1024]{3,2,1,0:T(8,128)(2,1)} collective-permute-done((bf16[1,2,256,1024]{3,2,1,0:T(8,128)(2,1)}, bf16[1,2,256,1024]{3,2,1,0:T(8,128)(2,1)}, u32[]{:S(2)}, u32[]{:S(2)}) %collective-permute-start.4) | collective-permute-done | bytes 1048608 | tf_op jit(solution)/shard_map/ppermute | solution.py:157
  92.2 2.3 %constant_dynamic-update-slice_fusion = bf16[1,2,256,4096]{3,2,1,0:T(8,128)(2,1)} fusion(bf16[1,2,256,4096]{3,2,1,0:T(8,128)(2,1)} %constant_dynamic-update-slice_fusion.1, bf16[1,2,256,1024]{3,2,1,0:T(8,128)(2,1)} %collective-permute-done.4, s32[]{:T(128)S(6)} %select_n.214), kind=kLoop, calls=%fused_computation.191 | loop fusion | bytes 2097156 | tf_op jit(solution)/shard_map/dynamic_update_slice | solution.py:158
  94.6 7.1 %all-gather.3.cloned.1.call-done = bf16[3,2,2048,512]{3,2,1,0:T(8,128)(2,1)} async-done(((bf16[3,2,64,512]{3,2,1,0:T(8,128)(2,1)}), bf16[3,2,2048,512]{3,2,1,0:T(8,128)(2,1)}) %all-gather.3.cloned.1.call-update) | async-done | bytes 12582928 | tf_op jit(solution)/shard_map/all_gather | solution.py:142
  101.7 11.7 %convolution_convert_fusion = bf16[3,512,512]{1,2,0:T(8,128)(2,1)} fusion(bf16[512,4096,1]{1,0,2:T(8,128)(2,1)} %bitcast.17, bf16[3,4096,512]{2,1,0:T(8,128)(2,1)} %bitcast.170), kind=kOutput, calls=%fused_computation.51 | convolution fusion | flops 6443237376 | bytes 18350080 | tf_op jit(solution)/shard_map/pdc,ld->pcl/dot_general | solution.py:165
  113.4 1.3 slice.382
  114.8 1.5 collective-permute-start.6
  116.3 0.5 copy.26
  117.1 0.3 copy.25
  117.5 0.7 maximum_convert_fusion
  118.1 1.7 fusion.7
  119.9 0.9 copy.27
  120.8 8.4 %all-to-all-start = ((bf16[32,16,2,256]{3,1,2,0:T(8,128)(2,1)}), bf16[32,16,2,256]{3,1,2,0:T(8,128)(2,1)S(1)}, u32[]{:S(2)}, u32[]{:S(2)}) async-start(bf16[32,16,2,256]{3,1,2,0:T(8,128)(2,1)} %copy.27), calls=%async_computation | async-start | bytes 1048576 | tf_op jit(solution)/shard_map/all_to_all | solution.py:192
  129.2 1.1 slice.381
  130.3 0.8 copy-done
  131.1 3.0 %collective-permute-start.5 = (bf16[1,512,256]{1,2,0:T(8,128)(2,1)S(1)}, bf16[1,512,256]{1,2,0:T(8,128)(2,1)}, u32[]{:S(2)}, u32[]{:S(2)}) collective-permute-start(bf16[1,512,256]{1,2,0:T(8,128)(2,1)S(1)} %constant_dynamic-slice_fusion.3), channel_id=1, source_target_pairs={{0,128},{128,0},{1,129},{129,1},{2,130},{130,2},{3,131},{131,3},{4... | collective-permute-start | bytes 786440 | tf_op jit(solution)/shard_map/ppermute | solution.py:172
  134.1 0.9 slice_bitcast_fusion.30
  135.1 0.8 slice_bitcast_fusion.31
  135.8 8.7 %collective-permute-done.5 = bf16[1,512,256]{1,2,0:T(8,128)(2,1)} collective-permute-done((bf16[1,512,256]{1,2,0:T(8,128)(2,1)S(1)}, bf16[1,512,256]{1,2,0:T(8,128)(2,1)}, u32[]{:S(2)}, u32[]{:S(2)}) %collective-permute-start.5) | collective-permute-done | bytes 262176 | tf_op jit(solution)/shard_map/ppermute | solution.py:172
  144.5 1.3 all-to-all-done
  146.1 0.3 dot_general.19
  146.6 3.6 %fusion.4 = f32[16,16,2048]{2,1,0:T(8,128)S(1)} fusion(bf16[16,16,1024]{2,1,0:T(8,128)(2,1)S(1)} %dot_general.19, bf16[1024,2048]{1,0:T(8,128)(2,1)} %pad_maximum_fusion.1), kind=kOutput, calls=%fused_computation.40 | convolution fusion | flops 1073741824 | bytes 6815744 | tf_op jit(solution)/shard_map/dot_general | solution.py:69
  150.6 4.5 %subtract_convert_fusion.1 = bf16[16,16,1024]{2,1,0:T(8,128)(2,1)S(1)} fusion(f32[16,16,1024]{2,1,0:T(8,128)S(1)} %get-tuple-element.50, f32[16,1024]{1,0:T(8,128)S(1)} %copy-done.6, f32[16,1024]{1,0:T(8,128)S(1)} %copy-done.7, f32[16,1024]{1,0:T(8,128)S(1)} %copy-done.9, f32[16,1024]{1,0:T(8,128)S(1)} %copy-done.10, f32[16,1024]{1,0:T(8,128)S(1)} %copy-done.11, ...), kind=kLoop, calls=%fused_computation.75 | loop fusion | flops 17039360 | bytes 4719616 | tf_op jit(solution)/shard_map/convert.2 | solution.py:232
  155.2 5.2 %select_convert_fusion = bf16[16,16,1024]{2,1,0:T(8,128)(2,1)S(1)} fusion(f32[16,16,1024]{2,1,0:T(8,128)S(1)} %get-tuple-element.50, f32[16,16,1024]{2,1,0:T(8,128)S(1)} %get-tuple-element.49, f32[16,1024]{1,0:T(8,128)S(1)} %get-tuple-element.18, f32[16,1024]{1,0:T(8,128)S(1)} %get-tuple-element.19, f32[16,1024]{1,0:T(8,128)S(1)} %get-tuple-element.20, ...), kind=kLoop, calls=%fused_computation.74 | loop fusion | flops 25165824 | bytes 4719616 | tf_op jit(solution)/shard_map/convert.3 | solution.py:232
  160.6 2.4 %fusion = f32[16,16,2048]{2,1,0:T(8,128)S(1)} fusion(bf16[2048,2048]{1,0:T(8,128)(2,1)S(1)} %bitcast.152, bf16[16,16,1024]{2,1,0:T(8,128)(2,1)S(1)} %select_convert_fusion, bf16[16,16,1024]{2,1,0:T(8,128)(2,1)S(1)} %subtract_convert_fusion.1), kind=kOutput, calls=%fused_computation.1 | convolution fusion | flops 2149580800 | bytes 11534336 | tf_op jit(solution)/shard_map/dot_general | solution.py:90
  163.7 1.4 fusion.22
  165.2 8.8 %all-to-all-start.1 = ((bf16[64,16,256]{2,1,0:T(8,128)(2,1)}), bf16[64,16,256]{2,1,0:T(8,128)(2,1)S(1)}, u32[]{:S(2)}, u32[]{:S(2)}) async-start(bf16[64,16,256]{2,1,0:T(8,128)(2,1)} %bitcast.62), calls=%async_computation.1 | async-start | bytes 1048576 | tf_op jit(solution)/shard_map/all_to_all | solution.py:202
  174.0 1.0 broadcast_select_fusion
  175.1 3.5 %collective-permute-start.7 = (bf16[1,1024,2]{1,2,0:T(2,128)(2,1)S(1)}, bf16[1,1024,2]{1,2,0:T(2,128)(2,1)S(1)}, u32[]{:S(2)}, u32[]{:S(2)}) collective-permute-start(bf16[1,1024,2]{1,2,0:T(2,128)(2,1)S(1)} %fusion.60), channel_id=1, source_target_pairs={{0,4},{4,8},{8,12},{12,16},{16,20},{20,24},{24,28},{28,32},{32,36}... | collective-permute-start | bytes 12296 | tf_op jit(solution)/shard_map/ppermute | solution.py:15
  178.7 3.7 %collective-permute-done.7 = bf16[1,1024,2]{1,2,0:T(2,128)(2,1)S(1)} collective-permute-done((bf16[1,1024,2]{1,2,0:T(2,128)(2,1)S(1)}, bf16[1,1024,2]{1,2,0:T(2,128)(2,1)S(1)}, u32[]{:S(2)}, u32[]{:S(2)}) %collective-permute-start.7) | collective-permute-done | bytes 4128 | tf_op jit(solution)/shard_map/ppermute | solution.py:15
  182.4 9.0 %all-to-all-done.1 = bf16[64,16,256]{2,1,0:T(8,128)(2,1)S(1)} async-done(((bf16[64,16,256]{2,1,0:T(8,128)(2,1)}), bf16[64,16,256]{2,1,0:T(8,128)(2,1)S(1)}, u32[]{:S(2)}, u32[]{:S(2)}) %all-to-all-start.1) | async-done | bytes 524320 | tf_op jit(solution)/shard_map/all_to_all | solution.py:202
  191.6 0.3 copy.31
  191.9 0.4 fusion.15
  192.3 1.0 copy.32
  (88 shorter events, 2.9 us)
Async XLA Ops:
  6.5 95.1 %all-gather.3.cloned.1.call-start = ((), (), s32[]{:S(2)}) async-start(), calls=%async_computation.2 | async-start | bytes 12976128 | tf_op jit(solution)/shard_map/all_gather | solution.py:142
  7.5 7.4 %collective-permute-start = (bf16[3,64,512]{2,1,0:T(8,128)(2,1)S(1)}, bf16[3,64,512]{2,1,0:T(8,128)(2,1)S(1)}, u32[]{:S(2)}, u32[]{:S(2)}) collective-permute-start(bf16[3,64,512]{2,1,0:T(8,128)(2,1)S(1)} %constant_dynamic-slice_fusion.4), channel_id=1, source_target_pairs={{0,128},{128,0},{1,129},{129,1},{2,130},{130,2},{3,131},{131,3},{4... | collective-permute-start | bytes 589832 | tf_op jit(solution)/shard_map/ppermute | solution.py:140
  16.7 21.8 %collective-permute-start.1 = (bf16[256,1024]{1,0:T(8,128)(2,1)}, bf16[256,1024]{1,0:T(8,128)(2,1)S(1)}, u32[]{:S(2)}, u32[]{:S(2)}) collective-permute-start(bf16[256,1024]{1,0:T(8,128)(2,1)} %param.5), channel_id=1, source_target_pairs={{0,128},{128,0},{1,129},{129,1},{2,130},{130,2},{3,131},{131,3},{4... | collective-permute-start | bytes 1572872 | tf_op jit(solution)/shard_map/ppermute | solution.py:144
  35.6 2.8 %copy-start.21 = (bf16[256,1024]{1,0:T(8,128)(2,1)S(1)}, bf16[256,1024]{1,0:T(8,128)(2,1)}, u32[]{:S(2)}) copy-start(bf16[256,1024]{1,0:T(8,128)(2,1)} %param.5) | copy-start | bytes 1572868
  39.6 6.1 %slice-start.2 = ((f32[3,3,1024]{2,1,0:T(4,128)}), f32[2,3,1024]{2,1,0:T(4,128)S(1)}, s32[]{:S(2)}) async-start(f32[3,3,1024]{2,1,0:T(4,128)} %param.7), calls=%async_computation.5 | async-start | bytes 65536 | tf_op jit(solution)/shard_map/slice | solution.py:180
  39.6 23.2 %collective-permute-start.2 = (bf16[1,2,256,1024]{3,2,1,0:T(8,128)(2,1)}, bf16[1,2,256,1024]{3,2,1,0:T(8,128)(2,1)S(1)}, u32[]{:S(2)}, u32[]{:S(2)}) collective-permute-start(bf16[1,2,256,1024]{3,2,1,0:T(8,128)(2,1)} %maximum_bitcast_fusion), channel_id=1, source_target_pairs={{0,1},{1,0},{2,3},{3,2},{4,5},{5,4},{6,7},{7,6},{8,9},{9,8},{10,11... | collective-permute-start | bytes 3145736 | tf_op jit(solution)/shard_map/ppermute | solution.py:157
  43.3 44.2 %collective-permute-start.3 = (bf16[1,2,256,1024]{3,2,1,0:T(8,128)(2,1)}, bf16[1,2,256,1024]{3,2,1,0:T(8,128)(2,1)S(1)}, u32[]{:S(2)}, u32[]{:S(2)}) collective-permute-start(bf16[1,2,256,1024]{3,2,1,0:T(8,128)(2,1)} %maximum_bitcast_fusion), channel_id=1, source_target_pairs={{0,2},{1,3},{2,0},{3,1},{4,6},{5,7},{6,4},{7,5},{8,10},{9,11},{10,... | collective-permute-start | bytes 3145736 | tf_op jit(solution)/shard_map/ppermute | solution.py:157
  45.8 46.4 %collective-permute-start.4 = (bf16[1,2,256,1024]{3,2,1,0:T(8,128)(2,1)}, bf16[1,2,256,1024]{3,2,1,0:T(8,128)(2,1)}, u32[]{:S(2)}, u32[]{:S(2)}) collective-permute-start(bf16[1,2,256,1024]{3,2,1,0:T(8,128)(2,1)} %maximum_bitcast_fusion), channel_id=1, source_target_pairs={{0,3},{1,2},{2,1},{3,0},{4,7},{5,6},{6,5},{7,4},{8,11},{9,10},{10,... | collective-permute-start | bytes 3145736 | tf_op jit(solution)/shard_map/ppermute | solution.py:157
  114.8 2.3 %collective-permute-start.6 = (bf16[8,512]{1,0:T(8,128)(2,1)S(1)}, bf16[8,512]{1,0:T(8,128)(2,1)S(1)}, u32[]{:S(2)}, u32[]{:S(2)}) collective-permute-start(bf16[8,512]{1,0:T(8,128)(2,1)S(1)} %reshape.438), channel_id=1, source_target_pairs={{0,4},{4,8},{8,12},{12,16},{16,20},{20,24},{24,28},{28,32},{32,36}... | collective-permute-start | bytes 24584 | tf_op jit(solution)/shard_map/ppermute | solution.py:177
  119.8 14.3 %copy-start.2 = (f32[2048,256]{0,1:T(8,128)S(1)}, f32[2048,256]{0,1:T(8,128)}, u32[]{:S(2)}) copy-start(f32[2048,256]{0,1:T(8,128)} %fusion.67) | copy-start | bytes 6291460
  120.8 25.0 %all-to-all-start = ((bf16[32,16,2,256]{3,1,2,0:T(8,128)(2,1)}), bf16[32,16,2,256]{3,1,2,0:T(8,128)(2,1)S(1)}, u32[]{:S(2)}, u32[]{:S(2)}) async-start(bf16[32,16,2,256]{3,1,2,0:T(8,128)(2,1)} %copy.27), calls=%async_computation | async-start | bytes 1048576 | tf_op jit(solution)/shard_map/all_to_all | solution.py:192
  130.3 0.8 copy-start
  131.1 13.4 %collective-permute-start.5 = (bf16[1,512,256]{1,2,0:T(8,128)(2,1)S(1)}, bf16[1,512,256]{1,2,0:T(8,128)(2,1)}, u32[]{:S(2)}, u32[]{:S(2)}) collective-permute-start(bf16[1,512,256]{1,2,0:T(8,128)(2,1)S(1)} %constant_dynamic-slice_fusion.3), channel_id=1, source_target_pairs={{0,128},{128,0},{1,129},{129,1},{2,130},{130,2},{3,131},{131,3},{4... | collective-permute-start | bytes 786440 | tf_op jit(solution)/shard_map/ppermute | solution.py:172
  146.4 4.1 %copy-start.3 = (f32[16,1024]{1,0:T(8,128)S(1)}, f32[16,1024]{1,0:T(8,128)}, u32[]{:S(2)}) copy-start(f32[16,1024]{1,0:T(8,128)} %get-tuple-element.31) | copy-start | bytes 196612
  146.4 4.1 %copy-start.4 = (f32[16,1024]{1,0:T(8,128)S(1)}, f32[16,1024]{1,0:T(8,128)}, u32[]{:S(2)}) copy-start(f32[16,1024]{1,0:T(8,128)} %get-tuple-element.32) | copy-start | bytes 196612
  146.4 4.1 %copy-start.5 = (f32[16,1024]{1,0:T(8,128)S(1)}, f32[16,1024]{1,0:T(8,128)}, u32[]{:S(2)}) copy-start(f32[16,1024]{1,0:T(8,128)} %get-tuple-element.33) | copy-start | bytes 196612
  146.4 4.1 %copy-start.6 = (f32[16,1024]{1,0:T(8,128)S(1)}, f32[16,1024]{1,0:T(8,128)}, u32[]{:S(2)}) copy-start(f32[16,1024]{1,0:T(8,128)} %get-tuple-element.34) | copy-start | bytes 196612
  146.4 4.1 %copy-start.7 = (f32[16,1024]{1,0:T(8,128)S(1)}, f32[16,1024]{1,0:T(8,128)}, u32[]{:S(2)}) copy-start(f32[16,1024]{1,0:T(8,128)} %get-tuple-element.35) | copy-start | bytes 196612
  146.4 4.1 %copy-start.8 = (f32[16,1024]{1,0:T(8,128)S(1)}, f32[16,1024]{1,0:T(8,128)}, u32[]{:S(2)}) copy-start(f32[16,1024]{1,0:T(8,128)} %get-tuple-element.36) | copy-start | bytes 196612
  146.5 4.1 %copy-start.9 = (f32[16,1024]{1,0:T(8,128)S(1)}, f32[16,1024]{1,0:T(8,128)}, u32[]{:S(2)}) copy-start(f32[16,1024]{1,0:T(8,128)} %get-tuple-element.37) | copy-start | bytes 196612
  146.5 4.1 %copy-start.10 = (f32[16,1024]{1,0:T(8,128)S(1)}, f32[16,1024]{1,0:T(8,128)}, u32[]{:S(2)}) copy-start(f32[16,1024]{1,0:T(8,128)} %get-tuple-element.38) | copy-start | bytes 196612
  146.5 4.1 %copy-start.11 = (f32[16,1024]{1,0:T(8,128)S(1)}, f32[16,1024]{1,0:T(8,128)}, u32[]{:S(2)}) copy-start(f32[16,1024]{1,0:T(8,128)} %get-tuple-element.39) | copy-start | bytes 196612
  146.5 4.1 %copy-start.12 = (f32[16,1024]{1,0:T(8,128)S(1)}, f32[16,1024]{1,0:T(8,128)}, u32[]{:S(2)}) copy-start(f32[16,1024]{1,0:T(8,128)} %get-tuple-element.40) | copy-start | bytes 196612
  146.5 4.1 %copy-start.13 = (f32[16,1024]{1,0:T(8,128)S(1)}, f32[16,1024]{1,0:T(8,128)}, u32[]{:S(2)}) copy-start(f32[16,1024]{1,0:T(8,128)} %get-tuple-element.41) | copy-start | bytes 196612
  146.5 4.1 %copy-start.14 = (f32[16,1024]{1,0:T(8,128)S(1)}, f32[16,1024]{1,0:T(8,128)}, u32[]{:S(2)}) copy-start(f32[16,1024]{1,0:T(8,128)} %get-tuple-element.42) | copy-start | bytes 196612
  146.5 4.1 %copy-start.15 = (f32[16,1024]{1,0:T(8,128)S(1)}, f32[16,1024]{1,0:T(8,128)}, u32[]{:S(2)}) copy-start(f32[16,1024]{1,0:T(8,128)} %get-tuple-element.43) | copy-start | bytes 196612
  146.5 4.1 %copy-start.16 = (f32[16,1024]{1,0:T(8,128)S(1)}, f32[16,1024]{1,0:T(8,128)}, u32[]{:S(2)}) copy-start(f32[16,1024]{1,0:T(8,128)} %get-tuple-element.44) | copy-start | bytes 196612
  146.5 4.1 %copy-start.17 = (f32[16,1024]{1,0:T(8,128)S(1)}, f32[16,1024]{1,0:T(8,128)}, u32[]{:S(2)}) copy-start(f32[16,1024]{1,0:T(8,128)} %get-tuple-element.45) | copy-start | bytes 196612
  146.5 4.1 %copy-start.18 = (f32[16,1024]{1,0:T(8,128)S(1)}, f32[16,1024]{1,0:T(8,128)}, u32[]{:S(2)}) copy-start(f32[16,1024]{1,0:T(8,128)} %get-tuple-element.46) | copy-start | bytes 196612
  146.6 4.1 %copy-start.19 = (f32[16,1024]{1,0:T(8,128)S(1)}, f32[16,1024]{1,0:T(8,128)}, u32[]{:S(2)}) copy-start(f32[16,1024]{1,0:T(8,128)} %get-tuple-element.47) | copy-start | bytes 196612
  146.6 4.1 %copy-start.20 = (f32[16,1024]{1,0:T(8,128)S(1)}, f32[16,1024]{1,0:T(8,128)}, u32[]{:S(2)}) copy-start(f32[16,1024]{1,0:T(8,128)} %get-tuple-element.48) | copy-start | bytes 196612
  150.2 10.4 %slice-start = ((s8[8388608]{0:T(1024)(128)(4,1)}), s8[4194304]{0:T(1024)(128)(4,1)S(1)}, s32[]{:S(2)}) async-start(s8[8388608]{0:T(1024)(128)(4,1)} %bitcast.151), calls=%async_computation.3 | async-start | bytes 8388608
  150.6 9.9 %slice-start.1 = ((s8[8388608]{0:T(1024)(128)(4,1)}), s8[4194304]{0:T(1024)(128)(4,1)S(1)}, s32[]{:S(2)}) async-start(s8[8388608]{0:T(1024)(128)(4,1)} %bitcast.151), calls=%async_computation.4 | async-start | bytes 8388608
  163.1 0.7 copy-start.23
  163.3 10.7 %copy-start.22 = (f32[3,3,1024]{2,1,0:T(4,128)S(1)}, f32[3,3,1024]{2,1,0:T(4,128)}, u32[]{:S(2)}) copy-start(f32[3,3,1024]{2,1,0:T(4,128)} %param.7) | copy-start | bytes 110596
  163.6 10.4 %copy-start.1 = (bf16[1,512,512]{1,2,0:T(8,128)(2,1)S(1)}, bf16[1,512,512]{1,2,0:T(8,128)(2,1)}, u32[]{:S(2)}) copy-start(bf16[1,512,512]{1,2,0:T(8,128)(2,1)} %copy-done) | copy-start | bytes 1572868
  165.2 26.3 %all-to-all-start.1 = ((bf16[64,16,256]{2,1,0:T(8,128)(2,1)}), bf16[64,16,256]{2,1,0:T(8,128)(2,1)S(1)}, u32[]{:S(2)}, u32[]{:S(2)}) async-start(bf16[64,16,256]{2,1,0:T(8,128)(2,1)} %bitcast.62), calls=%async_computation.1 | async-start | bytes 1048576 | tf_op jit(solution)/shard_map/all_to_all | solution.py:202
  175.1 7.4 %collective-permute-start.7 = (bf16[1,1024,2]{1,2,0:T(2,128)(2,1)S(1)}, bf16[1,1024,2]{1,2,0:T(2,128)(2,1)S(1)}, u32[]{:S(2)}, u32[]{:S(2)}) collective-permute-start(bf16[1,1024,2]{1,2,0:T(2,128)(2,1)S(1)} %fusion.60), channel_id=1, source_target_pairs={{0,4},{4,8},{8,12},{12,16},{16,20},{20,24},{24,28},{28,32},{32,36}... | collective-permute-start | bytes 12296 | tf_op jit(solution)/shard_map/ppermute | solution.py:15
Sparse Core Ops, SparseCore 0:
  16.8 84.8 all-gather.2
